TPU v7x, 512 devices: a whole 4x8x8 slice. The times are simulated.
512 devices in a mesh: ctx: 64 (over y, z_lo, core), dp: 8 (over z_hi, x).
Axes of the slice: x: 4, y: 8, z: 8 (z_hi: 2, z_lo: 4; z = z_hi * 4 + z_lo), core: 2. Of those that a mesh axis runs over, the one named last changes fastest.
Arguments:
- features: bfloat16 [8, 12288, 1536], P('dp', 'ctx'), may hold values from -6 to 6
- bottleneck: bfloat16 [8, 12288, 384], P('dp', 'ctx'), may hold values from -6 to 6
- node_noise: bfloat16 [8, 12288, 1536], P('dp', 'ctx'), may hold values from -6 to 6
- targets: bfloat16 [8, 12288, 1536], P('dp', 'ctx'), may hold values from -15 to 15
- entry_weight: bfloat16 [384, 1536], P('ctx'), may hold values from -0.3125 to 0.3125
- conv_filters: bfloat16 [3, 1536, 384], P(None, None, 'ctx'), may hold values from -0.09375 to 0.09375
- exit_weight: bfloat16 [384, 1536], P('ctx'), may hold values from -0.3125 to 0.3125
Outputs:
- blended: bfloat16 [8, 12288, 1536], P('dp', 'ctx')
- estimate: float32 [384, 1536], P('ctx')
All inputs are finite; a program needn't handle non-finite values.
Results may differ from a plain program's by a relative error of at most 0.015.
The roundings to bfloat16 on the way count: a program that leaves them out, or rounds other values in their place, can miss the bound.
Values may be sent and summed in bfloat16 or wider, within the bound.
No kernel may reach another device: no remote copies, remote signals or barrier semaphores. Data moves between devices by JAX's collectives and lax.ppermute only.
A program may use at most 64 MiB of HBM per device.

v0:
```python
import jax
import jax.numpy as jnp
from jax import lax
from jax.sharding import PartitionSpec as P

DILATION = 32
NOISE_SCALE = 0.1


def padded_2(cells, sides, width):
    for axis, dim in sides:
        count = lax.axis_size(axis)
        ends = count - 1
        head = lax.slice_in_dim(cells, 0, width, axis=dim)
        tail = lax.slice_in_dim(cells, cells.shape[dim] - width, cells.shape[dim], axis=dim)
        cells = jnp.concatenate(
            [
                lax.ppermute(tail, axis, [(i, (i + 1) % count) for i in range(ends)]),
                cells,
                lax.ppermute(head, axis, [((i + 1) % count, i) for i in range(ends)]),
            ],
            axis=dim,
        )
    return cells


def taps_for(padded, row_count, spacing, portion):
    summed = jnp.dot(padded[..., 0:row_count, :], portion[0], preferred_element_type=jnp.float32)
    summed = summed + jnp.dot(
        padded[..., spacing : spacing + row_count, :],
        portion[1],
        preferred_element_type=jnp.float32,
    )
    summed = summed + jnp.dot(
        padded[..., 2 * spacing : 2 * spacing + row_count, :],
        portion[2],
        preferred_element_type=jnp.float32,
    )
    return summed


def rows_for(left_side, portion):
    return jnp.dot(left_side, portion, preferred_element_type=jnp.float32)


def body(features, bottleneck, node_noise, targets, entry_weight, conv_filters, exit_weight):
    feats = features[0]
    bottle = bottleneck[0]
    jitter = node_noise[0]
    goal = targets[0].astype(jnp.float32)
    row_count = feats.shape[0]
    chan_count = feats.shape[1]
    spacing = DILATION
    baseline = feats.astype(jnp.float32) + rows_for(
        bottle, lax.all_gather(entry_weight, "ctx", axis=0, tiled=True)
    )
    offset_field = jitter.astype(jnp.float32) * NOISE_SCALE
    results = []
    for polarity in (1.0, -1.0):
        state = baseline + polarity * offset_field
        activated = jax.nn.gelu(state).astype(jnp.bfloat16)
        padded = padded_2(activated, (("ctx", 0),), spacing)
        mixed = taps_for(
            padded, row_count, spacing, lax.all_gather(conv_filters, "ctx", axis=2, tiled=True)
        )
        inner = jax.nn.gelu(mixed).astype(jnp.bfloat16)
        results.append(
            state + rows_for(inner, lax.all_gather(exit_weight, "ctx", axis=0, tiled=True))
        )
    upper = results[0]
    lower = results[1]
    blended = ((upper + lower) * 0.5).astype(jnp.bfloat16)[None]
    local_gap = jnp.sum((upper - lower) * (upper + lower - 2.0 * goal)) / (
        row_count * lax.axis_size("ctx") * chan_count
    )
    factor = lax.psum(local_gap, "ctx") / (2.0 * NOISE_SCALE)
    local_term = factor * lax.dot_general(
        bottle, jitter, (((0,), (0,)), ((), ())), preferred_element_type=jnp.float32
    )
    grouped = lax.psum(local_term, "dp")
    estimate = lax.psum_scatter(grouped, "ctx", scatter_dimension=0, tiled=True)
    return (blended, estimate)


def solution(mesh):
    return jax.shard_map(
        body,
        mesh=mesh,
        in_specs=(
            P("dp", "ctx", None),
            P("dp", "ctx", None),
            P("dp", "ctx", None),
            P("dp", "ctx", None),
            P("ctx", None),
            P(None, None, "ctx"),
            P("ctx", None),
        ),
        out_specs=(P("dp", "ctx", None), P("ctx", None)),
        check_vma=False,
    )
```

profile of v0, /device:TPU:8, one launch (start us, length us, event | category | flops | bytes accessed | tf_op | source)
XLA Modules:
  0.0 814.6 jit_solution(17729310585328299950)
XLA Ops:
  10.3 121.3 %all-gather.8.cloned.1.call-done = bf16[64,6,1536]{2,1,0:T(8,128)(2,1)} async-done(((bf16[1,6,1536]{2,1,0:T(8,128)(2,1)}), bf16[64,6,1536]{2,1,0:T(8,128)(2,1)}) %all-gather.8.cloned.1.call-update) | async-done | bytes 1179664 | tf_op jit(solution)/shard_map/all_gather | solution.py:55
  131.6 2.3 reshape.11
  133.9 3.4 fusion.18
  138.0 4.7 collective-permute-start.3
  142.8 1.9 collective-permute-start.2
  145.4 6.3 collective-permute-start.1
  153.6 95.8 %all-gather.10.cloned.1.call-done = bf16[64,6,1536]{2,1,0:T(8,128)(2,1)} async-done(((bf16[1,6,1536]{2,1,0:T(8,128)(2,1)}), bf16[64,6,1536]{2,1,0:T(8,128)(2,1)}) %all-gather.10.cloned.1.call-update) | async-done | bytes 1179664 | tf_op jit(solution)/shard_map/all_gather | solution.py:68
  249.4 3.1 reshape.13
  252.5 118.6 %all-gather.6.cloned.1.call-done = bf16[3,1536,384]{1,0,2:T(4,128)(2,1)} async-done(((bf16[3,1536,6]{1,0,2:T(4,128)(2,1)}), bf16[3,1536,384]{1,0,2:T(4,128)(2,1)}) %all-gather.6.cloned.1.call-update) | async-done | bytes 3538960 | tf_op jit(solution)/shard_map/all_gather | solution.py:64
  371.1 12.6 %fusion.103 = (bf16[1,1536,384]{1,0,2:T(2,128)(2,1)}, bf16[1,1536,384]{1,0,2:T(2,128)(2,1)}, bf16[1,1536,384]{1,0,2:T(2,128)(2,1)}) fusion(bf16[3,1536,384]{1,0,2:T(4,128)(2,1)} %all-gather.6.cloned.1.call-done), kind=kLoop, calls=%fused_computation.97 | loop fusion | bytes 7077888 | tf_op jit(solution)/shard_map/slice | solution.py:28
  383.7 5.6 copy.15
  389.8 6.5 copy.16
  396.4 2.5 fusion.21
  398.9 5.6 copy.14
  404.5 3.9 convolution_add_fusion
  410.1 2.2 fusion.23
  412.2 4.6 fusion.20
  417.4 119.0 %psum.14 = f32[]{:T(128)} all-reduce(f32[]{:T(128)S(6)} %div.6), channel_id=1, replica_groups=mesh['ctx'=64,'dp'=8] {'ctx'}, use_global_device_ids=true, to_apply=%region_1.0 | all-reduce | flops 1 | bytes 8 | tf_op jit(solution)/shard_map/psum | solution.py:76
  537.6 149.7 %fusion = f32[8,1536]{1,0:T(8,128)S(1)} fusion(f32[384,1536]{1,0:T(8,128)S(1)} %convolution_multiply_fusion), kind=kCustom, calls=%all-reduce-scatter | all-reduce-scatter fusion | flops 786433 | bytes 2410496
  687.3 2.0 collective-permute-start.19
  689.2 21.3 %collective-permute-start.10 = (f32[8,1536]{1,0:T(8,128)S(1)}, f32[8,1536]{1,0:T(8,128)S(1)}, u32[]{:S(2)}, u32[]{:S(2)}) collective-permute-start(f32[8,1536]{1,0:T(8,128)S(1)} %fusion), channel_id=1, source_target_pairs={{0,56},{8,64},{16,72},{24,80},{32,88},{40,96},{48,104},{56,112},{6... | collective-permute-start | bytes 147464
  710.5 5.5 collective-permute-start.11
  717.9 2.3 collective-permute-start.13
  721.6 5.7 collective-permute-start.15
  728.9 2.7 collective-permute-start.17
  733.1 2.0 collective-permute-start.4
  735.1 3.0 collective-permute-start.5
  738.1 2.7 collective-permute-start.6
  740.8 4.1 collective-permute-start.7
  744.9 1.9 collective-permute-start.8
  746.9 3.9 collective-permute-start.9
  755.6 52.5 %psum.16 = f32[6,1536]{1,0:T(8,128)} all-reduce(f32[6,1536]{1,0:T(8,128)S(1)} %constant_dynamic-slice_fusion), channel_id=1, replica_groups=mesh['ctx'=64,'dp'=8] {'dp'}, use_global_device_ids=true, to_apply=%region_2.0 | all-reduce | flops 9216 | bytes 73728 | tf_op jit(solution)/shard_map/psum | solution.py:80
  (55 shorter events, 19.5 us)
Async XLA Ops:
  7.2 126.7 %copy-start = (bf16[1,192,384]{2,1,0:T(8,128)(2,1)S(1)}, bf16[1,192,384]{2,1,0:T(8,128)(2,1)}, u32[]{:S(2)}) copy-start(bf16[1,192,384]{2,1,0:T(8,128)(2,1)} %param.8) | copy-start | bytes 442372
  7.2 124.4 %all-gather.8.cloned.1.call-start = ((), (), s32[]{:S(2)}) async-start(), calls=%async_computation.1 | async-start | bytes 1597440 | tf_op jit(solution)/shard_map/all_gather | solution.py:55
  7.9 241.5 %all-gather.10.cloned.1.call-start = ((), (), s32[]{:S(2)}) async-start(), calls=%async_computation.2 | async-start | bytes 1597440 | tf_op jit(solution)/shard_map/all_gather | solution.py:68
  8.7 362.4 %all-gather.6.cloned.1.call-start = ((), (), s32[]{:S(2)}) async-start(), calls=%async_computation | async-start | bytes 4792320 | tf_op jit(solution)/shard_map/all_gather | solution.py:64
  10.3 123.6 %copy-start.2 = (bf16[1,192,1536]{2,1,0:T(8,128)(2,1)S(1)}, bf16[1,192,1536]{2,1,0:T(8,128)(2,1)}, u32[]{:S(2)}) copy-start(bf16[1,192,1536]{2,1,0:T(8,128)(2,1)} %param.9) | copy-start | bytes 1769476
  137.3 115.2 %copy-start.4 = (bf16[192,1536]{1,0:T(8,128)(2,1)}, bf16[192,1536]{1,0:T(8,128)(2,1)S(1)}, u32[]{:S(2)}) copy-start(bf16[192,1536]{1,0:T(8,128)(2,1)S(1)} %get-tuple-element.8) | copy-start | bytes 1769476
  137.3 259.1 %copy-start.3 = (bf16[192,1536]{1,0:T(8,128)(2,1)}, bf16[192,1536]{1,0:T(8,128)(2,1)S(1)}, u32[]{:S(2)}) copy-start(bf16[192,1536]{1,0:T(8,128)(2,1)S(1)} %get-tuple-element.7) | copy-start | bytes 1769476
  138.0 258.3 %collective-permute-start.3 = (bf16[32,1536]{1,0:T(8,128)(2,1)}, bf16[32,1536]{1,0:T(8,128)(2,1)}, u32[]{:S(2)}, u32[]{:S(2)}) collective-permute-start(bf16[32,1536]{1,0:T(8,128)(2,1)} %get-tuple-element.10), channel_id=1, source_target_pairs={{8,0},{16,8},{24,16},{32,24},{40,32},{48,40},{56,48},{64,56},{72,6... | collective-permute-start | bytes 294920 | tf_op jit(solution)/shard_map/ppermute | solution.py:20
  142.8 261.7 %collective-permute-start.2 = (bf16[32,1536]{1,0:T(8,128)(2,1)}, bf16[32,1536]{1,0:T(8,128)(2,1)}, u32[]{:S(2)}, u32[]{:S(2)}) collective-permute-start(bf16[32,1536]{1,0:T(8,128)(2,1)} %get-tuple-element.9), channel_id=1, source_target_pairs={{0,8},{8,16},{16,24},{24,32},{32,40},{40,48},{48,56},{56,64},{64,7... | collective-permute-start | bytes 294920 | tf_op jit(solution)/shard_map/ppermute | solution.py:18
  145.4 264.7 %collective-permute-start.1 = (bf16[32,1536]{1,0:T(8,128)(2,1)}, bf16[32,1536]{1,0:T(8,128)(2,1)}, u32[]{:S(2)}, u32[]{:S(2)}) collective-permute-start(bf16[32,1536]{1,0:T(8,128)(2,1)} %get-tuple-element.12), channel_id=1, source_target_pairs={{8,0},{16,8},{24,16},{32,24},{40,32},{48,40},{56,48},{64,56},{72,6... | collective-permute-start | bytes 294920 | tf_op jit(solution)/shard_map/ppermute | solution.py:20
  151.7 260.5 %collective-permute-start = (bf16[32,1536]{1,0:T(8,128)(2,1)}, bf16[32,1536]{1,0:T(8,128)(2,1)S(1)}, u32[]{:S(2)}, u32[]{:S(2)}) collective-permute-start(bf16[32,1536]{1,0:T(8,128)(2,1)} %get-tuple-element.11), channel_id=1, source_target_pairs={{0,8},{8,16},{16,24},{24,32},{32,40},{40,48},{48,56},{56,64},{64,7... | collective-permute-start | bytes 294920 | tf_op jit(solution)/shard_map/ppermute | solution.py:18
  408.4 1.7 copy-start.5
  408.4 1.7 copy-start.6
  410.0 2.2 copy-start.1
  687.3 33.0 %collective-permute-start.19 = (f32[6,1536]{1,0:T(8,128)S(1)}, f32[6,1536]{1,0:T(8,128)S(1)}, u32[]{:S(2)}, u32[]{:S(2)}) collective-permute-start(f32[6,1536]{1,0:T(8,128)S(1)} %slice.58), channel_id=1, source_target_pairs={{0,128},{8,136},{16,144},{24,152},{32,160},{40,168},{48,176},{56,1... | collective-permute-start | bytes 110600
  689.2 32.3 %collective-permute-start.10 = (f32[8,1536]{1,0:T(8,128)S(1)}, f32[8,1536]{1,0:T(8,128)S(1)}, u32[]{:S(2)}, u32[]{:S(2)}) collective-permute-start(f32[8,1536]{1,0:T(8,128)S(1)} %fusion), channel_id=1, source_target_pairs={{0,56},{8,64},{16,72},{24,80},{32,88},{40,96},{48,104},{56,112},{6... | collective-permute-start | bytes 147464
  710.5 16.8 %collective-permute-start.11 = (f32[8,1536]{1,0:T(8,128)S(1)}, f32[8,1536]{1,0:T(8,128)S(1)}, u32[]{:S(2)}, u32[]{:S(2)}) collective-permute-start(f32[8,1536]{1,0:T(8,128)S(1)} %fusion), channel_id=1, source_target_pairs={{0,64},{8,72},{16,80},{24,88},{32,96},{40,104},{48,112},{56,120},{... | collective-permute-start | bytes 147464
  716.0 12.9 %collective-permute-start.12 = (f32[8,1536]{1,0:T(8,128)S(1)}, f32[8,1536]{1,0:T(8,128)S(1)}, u32[]{:S(2)}, u32[]{:S(2)}) collective-permute-start(f32[8,1536]{1,0:T(8,128)S(1)} %fusion), channel_id=1, source_target_pairs={{0,72},{8,80},{16,88},{24,96},{32,104},{40,112},{48,120},{56,128},... | collective-permute-start | bytes 147464
  717.9 13.8 %collective-permute-start.13 = (f32[8,1536]{1,0:T(8,128)S(1)}, f32[8,1536]{1,0:T(8,128)S(1)}, u32[]{:S(2)}, u32[]{:S(2)}) collective-permute-start(f32[8,1536]{1,0:T(8,128)S(1)} %fusion), channel_id=1, source_target_pairs={{0,80},{8,88},{16,96},{24,104},{32,112},{40,120},{48,128},{56,136}... | collective-permute-start | bytes 147464
  720.3 12.8 %collective-permute-start.14 = (f32[8,1536]{1,0:T(8,128)S(1)}, f32[8,1536]{1,0:T(8,128)S(1)}, u32[]{:S(2)}, u32[]{:S(2)}) collective-permute-start(f32[8,1536]{1,0:T(8,128)S(1)} %fusion), channel_id=1, source_target_pairs={{0,88},{8,96},{16,104},{24,112},{32,120},{40,128},{48,136},{56,144... | collective-permute-start | bytes 147464
  721.6 13.5 %collective-permute-start.15 = (f32[8,1536]{1,0:T(8,128)S(1)}, f32[8,1536]{1,0:T(8,128)S(1)}, u32[]{:S(2)}, u32[]{:S(2)}) collective-permute-start(f32[8,1536]{1,0:T(8,128)S(1)} %fusion), channel_id=1, source_target_pairs={{0,96},{8,104},{16,112},{24,120},{32,128},{40,136},{48,144},{56,15... | collective-permute-start | bytes 147464
  727.3 10.8 %collective-permute-start.16 = (f32[8,1536]{1,0:T(8,128)S(1)}, f32[8,1536]{1,0:T(8,128)S(1)}, u32[]{:S(2)}, u32[]{:S(2)}) collective-permute-start(f32[8,1536]{1,0:T(8,128)S(1)} %fusion), channel_id=1, source_target_pairs={{0,104},{8,112},{16,120},{24,128},{32,136},{40,144},{48,152},{56,1... | collective-permute-start | bytes 147464
  728.9 11.9 %collective-permute-start.17 = (f32[8,1536]{1,0:T(8,128)S(1)}, f32[8,1536]{1,0:T(8,128)S(1)}, u32[]{:S(2)}, u32[]{:S(2)}) collective-permute-start(f32[8,1536]{1,0:T(8,128)S(1)} %fusion), channel_id=1, source_target_pairs={{0,112},{8,120},{16,128},{24,136},{32,144},{40,152},{48,160},{56,1... | collective-permute-start | bytes 147464
  731.7 13.2 %collective-permute-start.18 = (f32[8,1536]{1,0:T(8,128)S(1)}, f32[8,1536]{1,0:T(8,128)S(1)}, u32[]{:S(2)}, u32[]{:S(2)}) collective-permute-start(f32[8,1536]{1,0:T(8,128)S(1)} %fusion), channel_id=1, source_target_pairs={{0,120},{8,128},{16,136},{24,144},{32,152},{40,160},{48,168},{56,1... | collective-permute-start | bytes 147464
  733.1 13.8 %collective-permute-start.4 = (f32[8,1536]{1,0:T(8,128)S(1)}, f32[8,1536]{1,0:T(8,128)S(1)}, u32[]{:S(2)}, u32[]{:S(2)}) collective-permute-start(f32[8,1536]{1,0:T(8,128)S(1)} %fusion), channel_id=1, source_target_pairs={{0,8},{8,16},{16,24},{24,32},{32,40},{40,48},{48,56},{56,64},{64,7... | collective-permute-start | bytes 147464
  735.1 17.6 %collective-permute-start.5 = (f32[8,1536]{1,0:T(8,128)S(1)}, f32[8,1536]{1,0:T(8,128)S(1)}, u32[]{:S(2)}, u32[]{:S(2)}) collective-permute-start(f32[8,1536]{1,0:T(8,128)S(1)} %fusion), channel_id=1, source_target_pairs={{0,16},{8,24},{16,32},{24,40},{32,48},{40,56},{48,64},{56,72},{64,... | collective-permute-start | bytes 147464
  738.1 14.7 %collective-permute-start.6 = (f32[8,1536]{1,0:T(8,128)S(1)}, f32[8,1536]{1,0:T(8,128)S(1)}, u32[]{:S(2)}, u32[]{:S(2)}) collective-permute-start(f32[8,1536]{1,0:T(8,128)S(1)} %fusion), channel_id=1, source_target_pairs={{0,24},{8,32},{16,40},{24,48},{32,56},{40,64},{48,72},{56,80},{64,... | collective-permute-start | bytes 147464
  740.8 11.9 %collective-permute-start.7 = (f32[8,1536]{1,0:T(8,128)S(1)}, f32[8,1536]{1,0:T(8,128)S(1)}, u32[]{:S(2)}, u32[]{:S(2)}) collective-permute-start(f32[8,1536]{1,0:T(8,128)S(1)} %fusion), channel_id=1, source_target_pairs={{0,32},{8,40},{16,48},{24,56},{32,64},{40,72},{48,80},{56,88},{64,... | collective-permute-start | bytes 147464
  744.9 7.8 collective-permute-start.8
  746.9 6.9 collective-permute-start.9
Sparse Core Ops, SparseCore 0:
  10.2 121.3 all-gather.7
  133.7 115.6 all-gather.9
  251.6 119.4 all-gather.5
where the time goes:
time: 816 us; the launch traced here: 815 us
  waiting for transfers between devices  338 us (41%)
  blocking collectives  321 us (39%)
  starting transfers between devices  78.3 us (10%)
  local copies, waits for them, and re-layouts  41.9 us (5%)
  matrix products  19.1 us (2%)
  between operations  16.1 us (2%)
    unnamed x1, blocking collectives  150 us
    all_gather x1, waiting for transfers between devices, body(): lax.all_gather(entry_weight, 'ctx', axis=0, tiled=True)  121 us
    psum x1, blocking collectives, body(): factor = lax.psum(local_gap, 'ctx') / (2.0 * NOISE_SCALE)  119 us
    all_gather x1, waiting for transfers between devices, body(): lax.all_gather(conv_filters, 'ctx', axis=2, tiled=True)  119 us
    all_gather x1, waiting for transfers between devices, body(): lax.all_gather(exit_weight, 'ctx', axis=0, tiled=True)  95.8 us
    unnamed x16, starting transfers between devices  63.3 us
    psum x1, blocking collectives, body(): grouped = lax.psum(local_term, 'dp')  52.5 us
    unnamed x24, local copies, waits for them, and re-layouts  27.9 us
  transfers between devices with their start and end apart: 23, of which 4 were waited for; matrix products, arithmetic and copies ran while one was open for 7% of the time, Pallas kernels for 0%

commit v1 on v0

--- a/solution.py
+++ b/solution.py
@@ -51,9 +51,14 @@
     row_count = feats.shape[0]
     chan_count = feats.shape[1]
     spacing = DILATION
-    baseline = feats.astype(jnp.float32) + rows_for(
-        bottle, lax.all_gather(entry_weight, "ctx", axis=0, tiled=True)
-    )
+
+    def connect_cubes(page):
+        taken_in = jnp.concatenate(
+            lax.all_to_all(jnp.stack([page] * lax.axis_size("ctx")), "ctx", 0, 0), 0
+        )
+        return taken_in
+
+    baseline = feats.astype(jnp.float32) + rows_for(bottle, connect_cubes(entry_weight))
     offset_field = jitter.astype(jnp.float32) * NOISE_SCALE
     results = []
     for polarity in (1.0, -1.0):

time: 816 us -> 722 us (0.88)
  waiting for transfers between devices: 338 us -> 189 us
  blocking collectives: 321 us -> 376 us
    all_gather x1 -> x0, waiting for transfers between devices: 121 us -> none  [body(): lax.all_gather(entry_weight, 'ctx', axis=0, tiled=True)]
    all_to_all x0 -> x1, blocking collectives: none -> 54.7 us  [connect_cubes(): lax.all_to_all(jnp.stack([page] * lax.axis_size('ctx')), 'ctx', 0, 0)]
    all_gather x1, waiting for transfers between devices: 95.8 us -> 65.7 us  [body(): lax.all_gather(exit_weight, 'ctx', axis=0, tiled=True)]
    unnamed x24 -> x23, local copies, waits for them, and re-layouts: 27.9 us -> 25.6 us
  transfers between devices with their start and end apart: 23 -> 22, of which waited for: 4 -> 3; matrix products, arithmetic and copies ran while one was open for 7% -> 8% of each run, Pallas kernels for 0% -> 0%
where the time goes in v1:
time: 722 us; the launch traced here: 720 us
  blocking collectives  376 us (52%)
  waiting for transfers between devices  189 us (26%)
  starting transfers between devices  77.2 us (11%)
  local copies, waits for them, and re-layouts  41.7 us (6%)
  matrix products  19.5 us (3%)
  between operations  16.4 us (2%)
    unnamed x1, blocking collectives  150 us
    all_gather x1, waiting for transfers between devices, body(): lax.all_gather(conv_filters, 'ctx', axis=2, tiled=True)  122 us
    psum x1, blocking collectives, body(): factor = lax.psum(local_gap, 'ctx') / (2.0 * NOISE_SCALE)  119 us
    all_gather x1, waiting for transfers between devices, body(): lax.all_gather(exit_weight, 'ctx', axis=0, tiled=True)  65.7 us
    unnamed x16, starting transfers between devices  63.3 us
    all_to_all x1, blocking collectives, connect_cubes(): lax.all_to_all(jnp.stack([page] * lax.axis_size('ctx')), 'ctx', 0, 0)  54.7 us
    psum x1, blocking collectives, body(): grouped = lax.psum(local_term, 'dp')  52.5 us
    unnamed x23, local copies, waits for them, and re-layouts  25.6 us
  transfers between devices with their start and end apart: 22, of which 3 were waited for; matrix products, arithmetic and copies ran while one was open for 8% of the time, Pallas kernels for 0%

profile of v1, /device:TPU:8, one launch (start us, length us, event | category | flops | bytes accessed | tf_op | source)
XLA Modules:
  0.0 720.0 jit_solution(3280021906698806769)
XLA Ops:
  10.4 54.7 %all_to_all.5 = bf16[64,6,1536]{2,1,0:T(8,128)(2,1)S(1)} all-to-all(bf16[64,6,1536]{2,1,0:T(8,128)(2,1)S(1)} %stack.2), channel_id=1, replica_groups=mesh['ctx'=64,'dp'=8] {'ctx'}, dimensions={0} | all-to-all | bytes 2359296 | tf_op jit(solution)/shard_map/all_to_all | solution.py:57
  66.3 3.8 fusion.18
  70.8 3.6 collective-permute-start.3
  74.4 1.9 collective-permute-start.2
  77.0 6.3 collective-permute-start.1
  83.4 1.9 collective-permute-start
  85.3 65.7 %all-gather.6.cloned.1.call-done = bf16[64,6,1536]{2,1,0:T(8,128)(2,1)} async-done(((bf16[1,6,1536]{2,1,0:T(8,128)(2,1)}), bf16[64,6,1536]{2,1,0:T(8,128)(2,1)}) %all-gather.6.cloned.1.call-update) | async-done | bytes 1179664 | tf_op jit(solution)/shard_map/all_gather | solution.py:73
  151.0 3.1 reshape.17
  154.1 122.0 %all-gather.4.cloned.1.call-done = bf16[3,1536,384]{1,0,2:T(4,128)(2,1)} async-done(((bf16[3,1536,6]{1,0,2:T(4,128)(2,1)}), bf16[3,1536,384]{1,0,2:T(4,128)(2,1)}) %all-gather.4.cloned.1.call-update) | async-done | bytes 3538960 | tf_op jit(solution)/shard_map/all_gather | solution.py:69
  276.1 12.7 %fusion.103 = (bf16[1,1536,384]{1,0,2:T(2,128)(2,1)}, bf16[1,1536,384]{1,0,2:T(2,128)(2,1)}, bf16[1,1536,384]{1,0,2:T(2,128)(2,1)}) fusion(bf16[3,1536,384]{1,0,2:T(4,128)(2,1)} %all-gather.4.cloned.1.call-done), kind=kLoop, calls=%fused_computation.97 | loop fusion | bytes 7077888 | tf_op jit(solution)/shard_map/slice | solution.py:28
  288.8 5.6 copy.15
  294.9 6.5 copy.16
  301.4 2.5 fusion.21
  303.9 5.6 copy.14
  309.6 3.9 convolution_add_fusion
  315.1 2.2 fusion.23
  317.3 4.6 fusion.20
  322.5 119.0 %psum.14 = f32[]{:T(128)} all-reduce(f32[]{:T(128)S(6)} %div.6), channel_id=1, replica_groups=mesh['ctx'=64,'dp'=8] {'ctx'}, use_global_device_ids=true, to_apply=%region_1.0 | all-reduce | flops 1 | bytes 8 | tf_op jit(solution)/shard_map/psum | solution.py:81
  442.6 149.7 %fusion = f32[8,1536]{1,0:T(8,128)S(1)} fusion(f32[384,1536]{1,0:T(8,128)S(1)} %convolution_multiply_fusion), kind=kCustom, calls=%all-reduce-scatter | all-reduce-scatter fusion | flops 786433 | bytes 2410496
  592.3 2.0 collective-permute-start.19
  594.4 21.2 %collective-permute-start.10 = (f32[8,1536]{1,0:T(8,128)S(1)}, f32[8,1536]{1,0:T(8,128)S(1)}, u32[]{:S(2)}, u32[]{:S(2)}) collective-permute-start(f32[8,1536]{1,0:T(8,128)S(1)} %fusion), channel_id=1, source_target_pairs={{0,56},{8,64},{16,72},{24,80},{32,88},{40,96},{48,104},{56,112},{6... | collective-permute-start | bytes 147464
  615.5 5.5 collective-permute-start.11
  622.9 2.4 collective-permute-start.13
  626.6 5.7 collective-permute-start.15
  634.0 2.7 collective-permute-start.17
  638.2 2.0 collective-permute-start.4
  640.1 3.0 collective-permute-start.5
  643.1 2.7 collective-permute-start.6
  645.9 4.1 collective-permute-start.7
  650.0 1.9 collective-permute-start.8
  651.9 3.9 collective-permute-start.9
  660.7 52.5 %psum.16 = f32[6,1536]{1,0:T(8,128)} all-reduce(f32[6,1536]{1,0:T(8,128)S(1)} %constant_dynamic-slice_fusion), channel_id=1, replica_groups=mesh['ctx'=64,'dp'=8] {'dp'}, use_global_device_ids=true, to_apply=%region_2.0 | all-reduce | flops 9216 | bytes 73728 | tf_op jit(solution)/shard_map/psum | solution.py:85
  (54 shorter events, 18.9 us)
Async XLA Ops:
  7.2 59.1 %copy-start = (bf16[1,192,384]{2,1,0:T(8,128)(2,1)S(1)}, bf16[1,192,384]{2,1,0:T(8,128)(2,1)}, u32[]{:S(2)}) copy-start(bf16[1,192,384]{2,1,0:T(8,128)(2,1)} %param.8) | copy-start | bytes 442372
  7.2 143.8 %all-gather.6.cloned.1.call-start = ((), (), s32[]{:S(2)}) async-start(), calls=%async_computation.2 | async-start | bytes 1597440 | tf_op jit(solution)/shard_map/all_gather | solution.py:73
  7.9 268.2 %all-gather.4.cloned.1.call-start = ((), (), s32[]{:S(2)}) async-start(), calls=%async_computation.1 | async-start | bytes 4792320 | tf_op jit(solution)/shard_map/all_gather | solution.py:69
  65.1 1.2 copy-start.2
  70.0 84.1 %copy-start.4 = (bf16[192,1536]{1,0:T(8,128)(2,1)}, bf16[192,1536]{1,0:T(8,128)(2,1)S(1)}, u32[]{:S(2)}) copy-start(bf16[192,1536]{1,0:T(8,128)(2,1)S(1)} %get-tuple-element.8) | copy-start | bytes 1769476
  70.0 231.4 %copy-start.3 = (bf16[192,1536]{1,0:T(8,128)(2,1)}, bf16[192,1536]{1,0:T(8,128)(2,1)S(1)}, u32[]{:S(2)}) copy-start(bf16[192,1536]{1,0:T(8,128)(2,1)S(1)} %get-tuple-element.7) | copy-start | bytes 1769476
  70.8 230.7 %collective-permute-start.3 = (bf16[32,1536]{1,0:T(8,128)(2,1)}, bf16[32,1536]{1,0:T(8,128)(2,1)}, u32[]{:S(2)}, u32[]{:S(2)}) collective-permute-start(bf16[32,1536]{1,0:T(8,128)(2,1)} %get-tuple-element.10), channel_id=1, source_target_pairs={{8,0},{16,8},{24,16},{32,24},{40,32},{48,40},{56,48},{64,56},{72,6... | collective-permute-start | bytes 294920 | tf_op jit(solution)/shard_map/ppermute | solution.py:20
  74.4 235.1 %collective-permute-start.2 = (bf16[32,1536]{1,0:T(8,128)(2,1)}, bf16[32,1536]{1,0:T(8,128)(2,1)}, u32[]{:S(2)}, u32[]{:S(2)}) collective-permute-start(bf16[32,1536]{1,0:T(8,128)(2,1)} %get-tuple-element.9), channel_id=1, source_target_pairs={{0,8},{8,16},{16,24},{24,32},{32,40},{40,48},{48,56},{56,64},{64,7... | collective-permute-start | bytes 294920 | tf_op jit(solution)/shard_map/ppermute | solution.py:18
  77.0 238.1 %collective-permute-start.1 = (bf16[32,1536]{1,0:T(8,128)(2,1)}, bf16[32,1536]{1,0:T(8,128)(2,1)}, u32[]{:S(2)}, u32[]{:S(2)}) collective-permute-start(bf16[32,1536]{1,0:T(8,128)(2,1)} %get-tuple-element.12), channel_id=1, source_target_pairs={{8,0},{16,8},{24,16},{32,24},{40,32},{48,40},{56,48},{64,56},{72,6... | collective-permute-start | bytes 294920 | tf_op jit(solution)/shard_map/ppermute | solution.py:20
  83.4 233.9 %collective-permute-start = (bf16[32,1536]{1,0:T(8,128)(2,1)}, bf16[32,1536]{1,0:T(8,128)(2,1)S(1)}, u32[]{:S(2)}, u32[]{:S(2)}) collective-permute-start(bf16[32,1536]{1,0:T(8,128)(2,1)} %get-tuple-element.11), channel_id=1, source_target_pairs={{0,8},{8,16},{16,24},{24,32},{32,40},{40,48},{48,56},{56,64},{64,7... | collective-permute-start | bytes 294920 | tf_op jit(solution)/shard_map/ppermute | solution.py:18
  313.4 1.7 copy-start.5
  313.4 1.7 copy-start.6
  315.1 2.2 copy-start.1
  592.3 33.0 %collective-permute-start.19 = (f32[6,1536]{1,0:T(8,128)S(1)}, f32[6,1536]{1,0:T(8,128)S(1)}, u32[]{:S(2)}, u32[]{:S(2)}) collective-permute-start(f32[6,1536]{1,0:T(8,128)S(1)} %slice.58), channel_id=1, source_target_pairs={{0,128},{8,136},{16,144},{24,152},{32,160},{40,168},{48,176},{56,1... | collective-permute-start | bytes 110600
  594.4 32.3 %collective-permute-start.10 = (f32[8,1536]{1,0:T(8,128)S(1)}, f32[8,1536]{1,0:T(8,128)S(1)}, u32[]{:S(2)}, u32[]{:S(2)}) collective-permute-start(f32[8,1536]{1,0:T(8,128)S(1)} %fusion), channel_id=1, source_target_pairs={{0,56},{8,64},{16,72},{24,80},{32,88},{40,96},{48,104},{56,112},{6... | collective-permute-start | bytes 147464
  615.5 16.8 %collective-permute-start.11 = (f32[8,1536]{1,0:T(8,128)S(1)}, f32[8,1536]{1,0:T(8,128)S(1)}, u32[]{:S(2)}, u32[]{:S(2)}) collective-permute-start(f32[8,1536]{1,0:T(8,128)S(1)} %fusion), channel_id=1, source_target_pairs={{0,64},{8,72},{16,80},{24,88},{32,96},{40,104},{48,112},{56,120},{... | collective-permute-start | bytes 147464
  621.0 13.0 %collective-permute-start.12 = (f32[8,1536]{1,0:T(8,128)S(1)}, f32[8,1536]{1,0:T(8,128)S(1)}, u32[]{:S(2)}, u32[]{:S(2)}) collective-permute-start(f32[8,1536]{1,0:T(8,128)S(1)} %fusion), channel_id=1, source_target_pairs={{0,72},{8,80},{16,88},{24,96},{32,104},{40,112},{48,120},{56,128},... | collective-permute-start | bytes 147464
  622.9 13.8 %collective-permute-start.13 = (f32[8,1536]{1,0:T(8,128)S(1)}, f32[8,1536]{1,0:T(8,128)S(1)}, u32[]{:S(2)}, u32[]{:S(2)}) collective-permute-start(f32[8,1536]{1,0:T(8,128)S(1)} %fusion), channel_id=1, source_target_pairs={{0,80},{8,88},{16,96},{24,104},{32,112},{40,120},{48,128},{56,136}... | collective-permute-start | bytes 147464
  625.3 12.8 %collective-permute-start.14 = (f32[8,1536]{1,0:T(8,128)S(1)}, f32[8,1536]{1,0:T(8,128)S(1)}, u32[]{:S(2)}, u32[]{:S(2)}) collective-permute-start(f32[8,1536]{1,0:T(8,128)S(1)} %fusion), channel_id=1, source_target_pairs={{0,88},{8,96},{16,104},{24,112},{32,120},{40,128},{48,136},{56,144... | collective-permute-start | bytes 147464
  626.6 13.5 %collective-permute-start.15 = (f32[8,1536]{1,0:T(8,128)S(1)}, f32[8,1536]{1,0:T(8,128)S(1)}, u32[]{:S(2)}, u32[]{:S(2)}) collective-permute-start(f32[8,1536]{1,0:T(8,128)S(1)} %fusion), channel_id=1, source_target_pairs={{0,96},{8,104},{16,112},{24,120},{32,128},{40,136},{48,144},{56,15... | collective-permute-start | bytes 147464
  632.3 10.8 %collective-permute-start.16 = (f32[8,1536]{1,0:T(8,128)S(1)}, f32[8,1536]{1,0:T(8,128)S(1)}, u32[]{:S(2)}, u32[]{:S(2)}) collective-permute-start(f32[8,1536]{1,0:T(8,128)S(1)} %fusion), channel_id=1, source_target_pairs={{0,104},{8,112},{16,120},{24,128},{32,136},{40,144},{48,152},{56,1... | collective-permute-start | bytes 147464
  634.0 11.9 %collective-permute-start.17 = (f32[8,1536]{1,0:T(8,128)S(1)}, f32[8,1536]{1,0:T(8,128)S(1)}, u32[]{:S(2)}, u32[]{:S(2)}) collective-permute-start(f32[8,1536]{1,0:T(8,128)S(1)} %fusion), channel_id=1, source_target_pairs={{0,112},{8,120},{16,128},{24,136},{32,144},{40,152},{48,160},{56,1... | collective-permute-start | bytes 147464
  636.8 13.2 %collective-permute-start.18 = (f32[8,1536]{1,0:T(8,128)S(1)}, f32[8,1536]{1,0:T(8,128)S(1)}, u32[]{:S(2)}, u32[]{:S(2)}) collective-permute-start(f32[8,1536]{1,0:T(8,128)S(1)} %fusion), channel_id=1, source_target_pairs={{0,120},{8,128},{16,136},{24,144},{32,152},{40,160},{48,168},{56,1... | collective-permute-start | bytes 147464
  638.2 13.8 %collective-permute-start.4 = (f32[8,1536]{1,0:T(8,128)S(1)}, f32[8,1536]{1,0:T(8,128)S(1)}, u32[]{:S(2)}, u32[]{:S(2)}) collective-permute-start(f32[8,1536]{1,0:T(8,128)S(1)} %fusion), channel_id=1, source_target_pairs={{0,8},{8,16},{16,24},{24,32},{32,40},{40,48},{48,56},{56,64},{64,7... | collective-permute-start | bytes 147464
  640.1 17.6 %collective-permute-start.5 = (f32[8,1536]{1,0:T(8,128)S(1)}, f32[8,1536]{1,0:T(8,128)S(1)}, u32[]{:S(2)}, u32[]{:S(2)}) collective-permute-start(f32[8,1536]{1,0:T(8,128)S(1)} %fusion), channel_id=1, source_target_pairs={{0,16},{8,24},{16,32},{24,40},{32,48},{40,56},{48,64},{56,72},{64,... | collective-permute-start | bytes 147464
  643.1 14.7 %collective-permute-start.6 = (f32[8,1536]{1,0:T(8,128)S(1)}, f32[8,1536]{1,0:T(8,128)S(1)}, u32[]{:S(2)}, u32[]{:S(2)}) collective-permute-start(f32[8,1536]{1,0:T(8,128)S(1)} %fusion), channel_id=1, source_target_pairs={{0,24},{8,32},{16,40},{24,48},{32,56},{40,64},{48,72},{56,80},{64,... | collective-permute-start | bytes 147464
  645.9 11.9 %collective-permute-start.7 = (f32[8,1536]{1,0:T(8,128)S(1)}, f32[8,1536]{1,0:T(8,128)S(1)}, u32[]{:S(2)}, u32[]{:S(2)}) collective-permute-start(f32[8,1536]{1,0:T(8,128)S(1)} %fusion), channel_id=1, source_target_pairs={{0,32},{8,40},{16,48},{24,56},{32,64},{40,72},{48,80},{56,88},{64,... | collective-permute-start | bytes 147464
  650.0 7.8 %collective-permute-start.8 = (f32[8,1536]{1,0:T(8,128)S(1)}, f32[8,1536]{1,0:T(8,128)S(1)}, u32[]{:S(2)}, u32[]{:S(2)}) collective-permute-start(f32[8,1536]{1,0:T(8,128)S(1)} %fusion), channel_id=1, source_target_pairs={{0,40},{8,48},{16,56},{24,64},{32,72},{40,80},{48,88},{56,96},{64,... | collective-permute-start | bytes 147464
  651.9 6.9 collective-permute-start.9
Sparse Core Ops, SparseCore 0:
  10.2 140.8 all-gather.5
  153.2 122.9 all-gather.3
